TPU v7x, 256 devices: a whole 4x4x8 slice. The times are simulated.
256 devices in a mesh: ctx: 64 (over x, y_hi, z), pipe: 4 (over y_lo, core).
Axes of the slice: x: 4, y: 4 (y_hi: 2, y_lo: 2; y = y_hi * 2 + y_lo), z: 8, core: 2. Of those that a mesh axis runs over, the one named last changes fastest.
Arguments:
- inputs: bfloat16 [4, 8192, 4096], P('pipe', 'ctx'), may hold values from -16 to 16
- q_raw: bfloat16 [4, 8192, 2048], P('pipe', 'ctx'), may hold values from -6 to 6
- grad_out: bfloat16 [4, 8192, 2048], P('pipe', 'ctx'), may hold values from -6 to 6
- segments: int32 [4, 8192], P('pipe'), may hold values from 0 to 4, never falling along the last dimension, each value on 1 to 3072 neighbouring positions
- w_key: bfloat16 [4, 4096, 512], P('pipe', 'ctx'), may hold values from -0.09375 to 0.09375
- w_value: bfloat16 [4, 4096, 512], P('pipe', 'ctx'), may hold values from -0.09375 to 0.09375
- q_gain: float32 [4, 128], P('pipe'), may hold values from 0.1 to 1.9
- k_gain: float32 [4, 128], P('pipe'), may hold values from 0.1 to 1.9
Outputs:
- query_grad: bfloat16 [4, 8192, 2048], P('pipe', 'ctx')
- key_weight_grad: float32 [4, 4096, 512], P('pipe', 'ctx')
- value_weight_grad: float32 [4, 4096, 512], P('pipe', 'ctx')
- section_grad: bfloat16 [4, 8192, 4096], P('pipe', 'ctx')
Inputs may be any that keep to these rules, and one draw needn't show every extreme that they name: `segments`: along each section's sequence the document numbers never fall; every document has 1 to 3072 tokens and one has exactly 3072.
All inputs are finite; a program needn't handle non-finite values.
Results may differ from a plain program's by a relative error of at most 0.019.
Values may be sent and summed in bfloat16 or wider, within the bound.
No kernel may reach another device: no remote copies, remote signals or barrier semaphores. Data moves between devices by JAX's collectives and lax.ppermute only.
A program may use at most 128 MiB of HBM per device.

v0:
```python
import jax
import jax.numpy as jnp
from jax import lax
import functools
from jax.sharding import Mesh, NamedSharding, PartitionSpec as P

HEAD = 128
WINDOW = 768
epsilon = 1e-06
theta_base = 1000000.0


def axis_count(axis):
    names = axis if isinstance(axis, tuple) else (axis,)
    count = 1
    for name in names:
        count *= lax.axis_size(name)
    return count


def passed_along(block, axis, distance):
    devices = range(axis_count(axis))
    route = [(i - distance, i) for i in devices if i - distance in devices]
    return lax.ppermute(block, axis, route)


def shifted(shard, axis, by):
    devices = axis_count(axis)
    return lax.ppermute(shard, axis, [(i, (i + by) % devices) for i in range(devices)])


def rope_tables(positions):
    half_width = HEAD // 2
    frequency = jnp.exp(
        jnp.arange(half_width, dtype=jnp.float32) * (-2.0 * jnp.log(jnp.float32(theta_base)) / HEAD)
    )
    angles = positions.astype(jnp.float32)[:, None] * frequency[None, :]
    return (jnp.cos(angles), jnp.sin(angles))


def rotate(values, cosine, sine_table):
    half_width = values.shape[-1] // 2
    front_half = values[..., :half_width]
    back_half = values[..., half_width:]
    cos_b = cosine[:, None, :]
    sin_b = sine_table[:, None, :]
    return jnp.concatenate(
        [front_half * cos_b - back_half * sin_b, back_half * cos_b + front_half * sin_b], -1
    )


def unrotate(upstream, cosine, sine_table):
    half_width = upstream.shape[-1] // 2
    front_half = upstream[..., :half_width]
    back_half = upstream[..., half_width:]
    cos_b = cosine[:, None, :]
    sin_b = sine_table[:, None, :]
    return jnp.concatenate(
        [front_half * cos_b + back_half * sin_b, back_half * cos_b - front_half * sin_b], -1
    )


def normalize(values, gain_row):
    inverse = lax.rsqrt(jnp.mean(values * values, -1, keepdims=True) + epsilon)
    return (values * inverse * gain_row, inverse)


def normalize_back(values, inverse, gain_row, upstream):
    scaled = upstream * gain_row
    cubed = inverse * inverse * inverse
    return inverse * scaled - values * cubed * jnp.mean(values * scaled, -1, keepdims=True)


def guarded(tile_work, operands):
    return tile_work(*operands)


def local(inputs, q_raw, grad_out, segments, w_key, w_value, q_gain, k_gain, row_parts, col_parts):
    tokens_here = inputs[0]
    tok_rows = tokens_here.shape[0]
    kv_width = w_key.shape[2]
    kv_heads = kv_width // HEAD
    q_heads = q_raw.shape[2] // HEAD
    group = q_heads // kv_heads
    score_scale = HEAD ** (-0.5)
    reach_blocks = WINDOW // tok_rows
    col_index = lax.axis_index("cz")
    ctx_index = lax.axis_index("cb") * col_parts + col_index
    both_rows = jnp.concatenate([w_key[0], w_value[0]], 1)
    weight_slice = lax.all_gather(both_rows, "cz", axis=0, tiled=True)
    inputs_slice = lax.all_to_all(tokens_here, "cb", 1, 0, tiled=True)
    projected = lax.psum_scatter(
        jnp.dot(inputs_slice, weight_slice, preferred_element_type=jnp.float32),
        "cb",
        scatter_dimension=0,
        tiled=True,
    )
    key_raw = projected[:, :kv_width].astype(jnp.bfloat16)
    value_own = projected[:, kv_width:].astype(jnp.bfloat16).reshape(tok_rows, kv_heads, HEAD)
    local_pos = jnp.arange(tok_rows, dtype=jnp.int32)
    positions = ctx_index * tok_rows + local_pos
    cosine, sine_table = rope_tables(positions)
    query_in = q_raw[0].astype(jnp.float32).reshape(tok_rows, q_heads, HEAD)
    query_norm, query_inv = normalize(query_in, q_gain[0])
    query_rot = rotate(query_norm, cosine, sine_table).astype(jnp.bfloat16)
    key_in = key_raw.astype(jnp.float32).reshape(tok_rows, kv_heads, HEAD)
    key_norm, key_inv = normalize(key_in, k_gain[0])
    key_rot = rotate(key_norm, cosine, sine_table).astype(jnp.bfloat16)
    own_pair = jnp.stack([key_rot, value_own])
    key_blocks = [own_pair]
    for distance in range(1, reach_blocks + 1):
        key_blocks.append(passed_along(own_pair, CTX, distance))
    seg_all = segments[0]
    seg_query = lax.dynamic_slice_in_dim(seg_all, ctx_index * tok_rows, tok_rows)
    allowed_list = []
    for distance in range(reach_blocks + 1):
        key_pos = (ctx_index - distance) * tok_rows + local_pos
        seg_key = lax.dynamic_slice_in_dim(
            seg_all, jnp.maximum(ctx_index - distance, 0) * tok_rows, tok_rows
        )
        offset = positions[:, None] - key_pos[None, :]
        allowed = (
            (offset >= 0)
            & (offset < WINDOW)
            & (key_pos >= 0)[None, :]
            & (seg_query[:, None] == seg_key[None, :])
        )
        allowed_list.append(allowed)
    q_group = query_rot.reshape(tok_rows, kv_heads, group, HEAD)
    out_grad = grad_out[0].reshape(tok_rows, kv_heads, group, HEAD)

    def exp_block(key_pair, allowed):
        scores = (
            jnp.einsum("qgrd,kgd->grqk", q_group, key_pair[0], preferred_element_type=jnp.float32)
            * score_scale
        )
        return jnp.where(allowed, jnp.exp(scores), 0.0)

    def total_block(key_pair, allowed):
        return jnp.sum(exp_block(key_pair, allowed), -1)

    zero_total = jnp.zeros((kv_heads, group, tok_rows), jnp.float32)
    row_total = zero_total
    for distance in range(reach_blocks + 1):
        row_total = row_total + guarded(total_block, (key_blocks[distance], allowed_list[distance]))

    def prob_block(key_pair, allowed):
        prob_tile = (exp_block(key_pair, allowed) / row_total[..., None]).astype(jnp.bfloat16)
        out_tile = jnp.einsum(
            "grqk,kgd->qgrd", prob_tile, key_pair[1], preferred_element_type=jnp.float32
        )
        return (prob_tile, out_tile)

    zero_query = jnp.zeros((tok_rows, kv_heads, group, HEAD), jnp.float32)
    prob_list = []
    attn_out = zero_query
    for distance in range(reach_blocks + 1):
        prob_tile, out_tile = guarded(prob_block, (key_blocks[distance], allowed_list[distance]))
        prob_list.append(prob_tile)
        attn_out = attn_out + out_tile
    row_delta = jnp.sum(out_grad.astype(jnp.float32) * attn_out, -1).transpose(1, 2, 0)[..., None]

    def grad_block(key_pair, prob_tile):
        prob_grad = jnp.einsum(
            "qgrd,kgd->grqk", out_grad, key_pair[1], preferred_element_type=jnp.float32
        )
        score_grad = (prob_tile.astype(jnp.float32) * (prob_grad - row_delta)).astype(jnp.bfloat16)
        value_grad = jnp.einsum(
            "grqk,qgrd->kgd", prob_tile, out_grad, preferred_element_type=jnp.float32
        )
        key_grad = (
            jnp.einsum("grqk,qgrd->kgd", score_grad, q_group, preferred_element_type=jnp.float32)
            * score_scale
        )
        query_part = (
            jnp.einsum(
                "grqk,kgd->qgrd", score_grad, key_pair[0], preferred_element_type=jnp.float32
            )
            * score_scale
        )
        return (query_part, jnp.stack([key_grad, value_grad]))

    zero_pair = jnp.zeros((2, tok_rows, kv_heads, HEAD), jnp.float32)
    query_rot_grad = zero_query
    kv_total = zero_pair
    for distance in range(reach_blocks + 1):
        query_part, kv_part = guarded(grad_block, (key_blocks[distance], prob_list[distance]))
        query_rot_grad = query_rot_grad + query_part
        if distance == 0:
            kv_total = kv_part
        else:
            returned = passed_along(kv_part.astype(jnp.bfloat16), CTX, -distance)
            kv_total = kv_total + returned.astype(jnp.float32)
    query_grad = normalize_back(
        query_in,
        query_inv,
        q_gain[0],
        unrotate(query_rot_grad.reshape(tok_rows, q_heads, HEAD), cosine, sine_table),
    )
    query_grad = query_grad.reshape(tok_rows, q_heads * HEAD).astype(jnp.bfloat16)
    key_back = normalize_back(key_in, key_inv, k_gain[0], unrotate(kv_total[0], cosine, sine_table))
    key_back = key_back.reshape(tok_rows, kv_width).astype(jnp.bfloat16)
    value_back = kv_total[1].reshape(tok_rows, kv_width).astype(jnp.bfloat16)
    both_back = jnp.concatenate([key_back, value_back], 1)
    group_back = lax.all_gather(both_back, "cb", axis=0, tiled=True)
    grad_rows = lax.psum_scatter(
        lax.dot_general(
            inputs_slice, group_back, (((0,), (0,)), ((), ())), preferred_element_type=jnp.float32
        ),
        "cz",
        scatter_dimension=0,
        tiled=True,
    )
    slice_grad = lax.dot_general(
        group_back, weight_slice, (((1,), (1,)), ((), ())), preferred_element_type=jnp.float32
    ).astype(jnp.bfloat16)
    input_grad = lax.all_to_all(slice_grad, "cb", 0, 1, tiled=True)
    passed = shifted(input_grad, "pipe", -1)
    return (
        query_grad[None],
        grad_rows[:, :kv_width][None],
        grad_rows[:, kv_width:][None],
        passed[None],
    )


CTX = ("cb", "cz")


def solution(mesh):
    col_parts = 8
    row_parts = mesh.shape["ctx"] // col_parts
    grid = mesh.devices.reshape(row_parts, col_parts, mesh.shape["pipe"])
    split_mesh = Mesh(grid, ("cb", "cz", "pipe"))
    rows = P("pipe", CTX, None)
    inner = jax.shard_map(
        functools.partial(local, row_parts=row_parts, col_parts=col_parts),
        mesh=split_mesh,
        in_specs=(rows, rows, rows, P("pipe", None), rows, rows, P("pipe", None), P("pipe", None)),
        out_specs=(rows, rows, rows, rows),
        check_vma=False,
    )
    placed = NamedSharding(mesh, P("pipe", "ctx", None))

    def run(*args):
        return tuple((lax.with_sharding_constraint(out, placed) for out in inner(*args)))

    return run
```

profile of v0, /device:TPU:1, one launch (start us, length us, event | category | flops | bytes accessed | tf_op | source)
XLA Modules:
  0.0 400.0 jit_solution(7884223318868163470)
XLA Ops:
  7.2 1.5 pad_maximum_fusion.11
  8.8 1.6 copy.260
  10.4 22.6 %all_to_all.38 = bf16[128,8,512]{0,2,1:T(8,128)(2,1)S(1)} all-to-all(bf16[128,8,512]{0,2,1:T(8,128)(2,1)S(1)} %bitcast.575), channel_id=1, replica_groups=mesh['cb'=8,'cz'=8,'pipe'=4] {'cb'}, dimensions={1} | all-to-all | bytes 2097152 | tf_op jit(solution)/shard_map/all_to_all | solution.py:91
  33.6 14.6 %all-gather.3.cloned.1.call-done = bf16[512,1024]{1,0:T(8,128)(2,1)} async-done(((bf16[64,1024]{1,0:T(8,128)(2,1)}), bf16[512,1024]{1,0:T(8,128)(2,1)}) %all-gather.3.cloned.1.call-update) | async-done | bytes 1048592 | tf_op jit(solution)/shard_map/all_gather | solution.py:90
  48.2 4.5 %convolution_bitcast_fusion = f32[1024,1024]{0,1:T(8,128)} fusion(bf16[512,1024]{1,0:T(8,128)(2,1)} %all-gather.3.cloned.1.call-done, bf16[1024,512]{1,0:T(8,128)(2,1)S(1)} %bitcast.586), kind=kOutput, calls=%fused_computation | convolution fusion | flops 1073741824 | bytes 6291456 | tf_op jit(solution)/shard_map/dot_general | solution.py:93
  52.9 0.9 copy-done.16
  54.8 0.7 multiply_multiply_fusion.2
  57.0 1.3 copy.266
  58.4 1.0 fusion.129
  60.4 1.1 fusion.110
  61.5 83.1 %reduce-scatter.5.cloned.1.call-done = f32[128,1024]{0,1:T(8,128)} async-done(((f32[1024,1024]{0,1:T(8,128)}), f32[128,1024]{0,1:T(8,128)}) %reduce-scatter.5.cloned.1.call-update) | async-done | bytes 524304 | tf_op jit(solution)/shard_map/reduce_scatter | solution.py:92
  144.7 1.1 convert.86
  147.6 3.2 collective-permute-start
  150.8 6.4 %collective-permute-start.2 = (bf16[2,128,4,128]{3,1,2,0:T(8,128)(2,1)S(1)}, bf16[2,128,4,128]{3,1,2,0:T(8,128)(2,1)S(1)}, u32[]{:S(2)}, u32[]{:S(2)}) collective-permute-start(bf16[2,128,4,128]{3,1,2,0:T(8,128)(2,1)S(1)} %pad_maximum_fusion.2), channel_id=1, source_target_pairs={{0,12},{4,16},{8,20},{12,24},{16,28},{20,32},{24,36},{28,40},{32,4... | collective-permute-start | bytes 786440 | tf_op jit(solution)/shard_map/ppermute | solution.py:24
  157.2 2.2 collective-permute-start.3
  159.4 6.2 %collective-permute-start.4 = (bf16[2,128,4,128]{3,1,2,0:T(8,128)(2,1)S(1)}, bf16[2,128,4,128]{3,1,2,0:T(8,128)(2,1)S(1)}, u32[]{:S(2)}, u32[]{:S(2)}) collective-permute-start(bf16[2,128,4,128]{3,1,2,0:T(8,128)(2,1)S(1)} %pad_maximum_fusion.2), channel_id=1, source_target_pairs={{0,20},{4,24},{8,28},{12,32},{16,36},{20,40},{24,44},{28,48},{32,5... | collective-permute-start | bytes 786440 | tf_op jit(solution)/shard_map/ppermute | solution.py:24
  165.6 6.1 %collective-permute-start.5 = (bf16[2,128,4,128]{3,1,2,0:T(8,128)(2,1)S(1)}, bf16[2,128,4,128]{3,1,2,0:T(8,128)(2,1)S(1)}, u32[]{:S(2)}, u32[]{:S(2)}) collective-permute-start(bf16[2,128,4,128]{3,1,2,0:T(8,128)(2,1)S(1)} %pad_maximum_fusion.2), channel_id=1, source_target_pairs={{0,24},{4,28},{8,32},{12,36},{16,40},{20,44},{24,48},{28,52},{32,5... | collective-permute-start | bytes 786440 | tf_op jit(solution)/shard_map/ppermute | solution.py:24
  172.2 3.4 collective-permute-start.1
  175.6 1.1 fusion.146
  177.9 8.5 %collective-permute-done.4 = bf16[2,128,4,128]{3,1,2,0:T(8,128)(2,1)S(1)} collective-permute-done((bf16[2,128,4,128]{3,1,2,0:T(8,128)(2,1)S(1)}, bf16[2,128,4,128]{3,1,2,0:T(8,128)(2,1)S(1)}, u32[]{:S(2)}, u32[]{:S(2)}) %collective-permute-start.4) | collective-permute-done | bytes 262176 | tf_op jit(solution)/shard_map/ppermute | solution.py:24
  186.9 12.1 %collective-permute-done.5 = bf16[2,128,4,128]{3,1,2,0:T(8,128)(2,1)S(1)} collective-permute-done((bf16[2,128,4,128]{3,1,2,0:T(8,128)(2,1)S(1)}, bf16[2,128,4,128]{3,1,2,0:T(8,128)(2,1)S(1)}, u32[]{:S(2)}, u32[]{:S(2)}) %collective-permute-start.5) | collective-permute-done | bytes 262176 | tf_op jit(solution)/shard_map/ppermute | solution.py:24
  199.8 1.0 divide_convert_fusion.4
  206.0 1.3 collective-permute-start.6
  208.0 1.3 collective-permute-start.7
  209.9 1.3 collective-permute-start.8
  211.9 1.3 collective-permute-start.9
  213.8 1.4 collective-permute-start.10
  216.8 1.3 collective-permute-start.11
  218.7 9.8 %collective-permute-done.7 = bf16[2,128,4,128]{3,1,2,0:T(8,128)(2,1)S(1)} collective-permute-done((bf16[2,128,4,128]{3,1,2,0:T(8,128)(2,1)S(1)}, bf16[2,128,4,128]{3,1,2,0:T(8,128)(2,1)S(1)}, u32[]{:S(2)}, u32[]{:S(2)}) %collective-permute-start.7) | collective-permute-done | bytes 262176 | tf_op jit(solution)/shard_map/ppermute | solution.py:24
  228.5 9.2 %collective-permute-done.8 = bf16[2,128,4,128]{3,1,2,0:T(8,128)(2,1)S(1)} collective-permute-done((bf16[2,128,4,128]{3,1,2,0:T(8,128)(2,1)S(1)}, bf16[2,128,4,128]{3,1,2,0:T(8,128)(2,1)S(1)}, u32[]{:S(2)}, u32[]{:S(2)}) %collective-permute-start.8) | collective-permute-done | bytes 262176 | tf_op jit(solution)/shard_map/ppermute | solution.py:24
  237.8 13.4 %collective-permute-done.11 = bf16[2,128,4,128]{3,1,2,0:T(8,128)(2,1)S(1)} collective-permute-done((bf16[2,128,4,128]{3,1,2,0:T(8,128)(2,1)S(1)}, bf16[2,128,4,128]{3,1,2,0:T(8,128)(2,1)S(1)}, u32[]{:S(2)}, u32[]{:S(2)}) %collective-permute-start.11) | collective-permute-done | bytes 262176 | tf_op jit(solution)/shard_map/ppermute | solution.py:24
  252.8 1.0 copy.336
  254.0 0.7 pad_maximum_fusion.10
  255.0 1.2 mul.517
  256.2 1.2 mul.518
  257.4 1.2 mul.597
  258.5 1.1 mul.598
  259.7 74.3 %all-gather.5.cloned.1.call-done = bf16[1024,1024]{0,1:T(8,128)(2,1)} async-done(((bf16[128,1024]{0,1:T(8,128)(2,1)}), bf16[1024,1024]{0,1:T(8,128)(2,1)}) %all-gather.5.cloned.1.call-update) | async-done | bytes 2097168 | tf_op jit(solution)/shard_map/all_gather | solution.py:205
  333.9 4.5 %convolution_bitcast_fusion.1 = f32[512,1024]{0,1:T(8,128)} fusion(bf16[1024,1024]{0,1:T(8,128)(2,1)} %all-gather.5.cloned.1.call-done, bf16[1024,512]{1,0:T(8,128)(2,1)} %bitcast.587), kind=kOutput, calls=%fused_computation.1 | convolution fusion | flops 1073741824 | bytes 5242880 | tf_op jit(solution)/shard_map/dot_general | solution.py:207
  338.4 2.9 copy.460
  342.7 2.3 fusion.97
  345.0 1.4 fusion.98
  346.4 1.3 fusion.99
  347.7 1.3 fusion.100
  349.0 1.4 convolution_add_fusion.1
  350.4 2.3 convolution_convert_fusion
  352.7 3.7 all-to-all-start.1
  356.5 3.0 fusion.12
  359.5 1.1 fusion.138
  360.5 1.6 copy.462
  362.1 2.4 copy.463
  364.5 2.8 multiply_add_fusion
  367.3 3.4 all-to-all-done.1
  370.8 1.1 copy.469
  371.9 2.8 collective-permute-start.12
  375.3 1.3 mul.602
  376.6 2.5 mul.603
  379.1 1.1 concatenate.52
  380.3 2.9 fusion.88
  383.2 5.1 %collective-permute-done.12 = bf16[128,4096]{1,0:T(8,128)(2,1)} collective-permute-done((bf16[128,4096]{1,0:T(8,128)(2,1)}, bf16[128,4096]{1,0:T(8,128)(2,1)}, u32[]{:S(2)}, u32[]{:S(2)}) %collective-permute-start.12) | collective-permute-done | bytes 1048608 | tf_op jit(solution)/shard_map/ppermute | solution.py:29
  388.3 1.0 fusion.139
  389.5 0.8 copy.338
  390.4 0.8 copy.339
  391.1 2.3 copy.472
  (214 shorter events, 22.5 us)
Async XLA Ops:
  7.2 41.1 %all-gather.3.cloned.1.call-start = ((), (), s32[]{:S(2)}) async-start(), calls=%async_computation.4 | async-start | bytes 1179648 | tf_op jit(solution)/shard_map/all_gather | solution.py:90
  8.8 135.9 %reduce-scatter.5.cloned.1.call-start = ((), (), s32[]{:S(2)}) async-start(), calls=%async_computation.5 | async-start | bytes 4718592 | tf_op jit(solution)/shard_map/reduce_scatter | solution.py:92
  33.6 19.2 %copy-start.29 = (bf16[8,128,512]{2,1,0:T(8,128)(2,1)}, bf16[8,128,512]{2,1,0:T(8,128)(2,1)S(1)}, u32[]{:S(2)}) copy-start(bf16[8,128,512]{2,1,0:T(8,128)(2,1)S(1)} %copy.261) | copy-start | bytes 3145732
  52.8 281.1 %all-gather.5.cloned.1.call-start = ((), (), s32[]{:S(2)}) async-start(), calls=%async_computation.6 | async-start | bytes 2359296 | tf_op jit(solution)/shard_map/all_gather | solution.py:205
  56.8 2.9 copy-start.51
  59.7 87.5 %copy-start.20 = (f32[128,64]{1,0:T(8,128)S(1)}, f32[128,64]{1,0:T(8,128)}, u32[]{:S(2)}) copy-start(f32[128,64]{1,0:T(8,128)} %copy-done.19) | copy-start | bytes 98308
  59.7 87.5 %copy-start.24 = (f32[128,64]{1,0:T(8,128)S(1)}, f32[128,64]{1,0:T(8,128)}, u32[]{:S(2)}) copy-start(f32[128,64]{1,0:T(8,128)} %copy-done.23) | copy-start | bytes 98308
  145.8 56.8 %copy-start.17 = (bf16[128,512]{0,1:T(8,128)(2,1)}, bf16[128,512]{0,1:T(8,128)(2,1)S(1)}, u32[]{:S(2)}) copy-start(bf16[128,512]{0,1:T(8,128)(2,1)S(1)} %slice.130) | copy-start | bytes 393220
  146.6 25.1 %copy-start.46 = (pred[128,128]{0,1:T(8,128)(4,1)S(1)}, pred[128,128]{0,1:T(8,128)(4,1)}, u32[]{:S(2)}) copy-start(pred[128,128]{0,1:T(8,128)(4,1)} %get-tuple-element.62) | copy-start | bytes 49156
  147.3 29.4 %copy-start.14 = (bf16[128,4,64]{2,0,1:T(8,128)(2,1)}, bf16[128,4,64]{2,0,1:T(8,128)(2,1)S(1)}, u32[]{:S(2)}) copy-start(bf16[128,4,64]{2,0,1:T(8,128)(2,1)S(1)} %get-tuple-element.35) | copy-start | bytes 196612
  147.5 29.2 %copy-start.45 = (pred[128,128]{0,1:T(8,128)(4,1)S(1)}, pred[128,128]{0,1:T(8,128)(4,1)}, u32[]{:S(2)}) copy-start(pred[128,128]{0,1:T(8,128)(4,1)} %get-tuple-element.59) | copy-start | bytes 49156
  147.6 24.5 %collective-permute-start = (bf16[2,128,4,128]{3,1,2,0:T(8,128)(2,1)S(1)}, bf16[2,128,4,128]{3,1,2,0:T(8,128)(2,1)S(1)}, u32[]{:S(2)}, u32[]{:S(2)}) collective-permute-start(bf16[2,128,4,128]{3,1,2,0:T(8,128)(2,1)S(1)} %pad_maximum_fusion.2), channel_id=1, source_target_pairs={{0,4},{4,8},{8,12},{12,16},{16,20},{20,24},{24,28},{28,32},{32,36}... | collective-permute-start | bytes 786440 | tf_op jit(solution)/shard_map/ppermute | solution.py:24
  150.8 25.9 %collective-permute-start.2 = (bf16[2,128,4,128]{3,1,2,0:T(8,128)(2,1)S(1)}, bf16[2,128,4,128]{3,1,2,0:T(8,128)(2,1)S(1)}, u32[]{:S(2)}, u32[]{:S(2)}) collective-permute-start(bf16[2,128,4,128]{3,1,2,0:T(8,128)(2,1)S(1)} %pad_maximum_fusion.2), channel_id=1, source_target_pairs={{0,12},{4,16},{8,20},{12,24},{16,28},{20,32},{24,36},{28,40},{32,4... | collective-permute-start | bytes 786440 | tf_op jit(solution)/shard_map/ppermute | solution.py:24
  157.2 20.4 %collective-permute-start.3 = (bf16[2,128,4,128]{3,1,2,0:T(8,128)(2,1)S(1)}, bf16[2,128,4,128]{3,1,2,0:T(8,128)(2,1)S(1)}, u32[]{:S(2)}, u32[]{:S(2)}) collective-permute-start(bf16[2,128,4,128]{3,1,2,0:T(8,128)(2,1)S(1)} %pad_maximum_fusion.2), channel_id=1, source_target_pairs={{0,16},{4,20},{8,24},{12,28},{16,32},{20,36},{24,40},{28,44},{32,4... | collective-permute-start | bytes 786440 | tf_op jit(solution)/shard_map/ppermute | solution.py:24
  159.4 27.1 %collective-permute-start.4 = (bf16[2,128,4,128]{3,1,2,0:T(8,128)(2,1)S(1)}, bf16[2,128,4,128]{3,1,2,0:T(8,128)(2,1)S(1)}, u32[]{:S(2)}, u32[]{:S(2)}) collective-permute-start(bf16[2,128,4,128]{3,1,2,0:T(8,128)(2,1)S(1)} %pad_maximum_fusion.2), channel_id=1, source_target_pairs={{0,20},{4,24},{8,28},{12,32},{16,36},{20,40},{24,44},{28,48},{32,5... | collective-permute-start | bytes 786440 | tf_op jit(solution)/shard_map/ppermute | solution.py:24
  165.6 33.4 %collective-permute-start.5 = (bf16[2,128,4,128]{3,1,2,0:T(8,128)(2,1)S(1)}, bf16[2,128,4,128]{3,1,2,0:T(8,128)(2,1)S(1)}, u32[]{:S(2)}, u32[]{:S(2)}) collective-permute-start(bf16[2,128,4,128]{3,1,2,0:T(8,128)(2,1)S(1)} %pad_maximum_fusion.2), channel_id=1, source_target_pairs={{0,24},{4,28},{8,32},{12,36},{16,40},{20,44},{24,48},{28,52},{32,5... | collective-permute-start | bytes 786440 | tf_op jit(solution)/shard_map/ppermute | solution.py:24
  172.1 5.4 %copy-start.44 = (pred[128,128]{0,1:T(8,128)(4,1)S(1)}, pred[128,128]{0,1:T(8,128)(4,1)}, u32[]{:S(2)}) copy-start(pred[128,128]{0,1:T(8,128)(4,1)} %get-tuple-element.60) | copy-start | bytes 49156
  172.1 33.2 %copy-start.39 = (bf16[2,128,4,128]{3,1,2,0:T(8,128)(2,1)}, bf16[2,128,4,128]{3,1,2,0:T(8,128)(2,1)S(1)}, u32[]{:S(2)}) copy-start(bf16[2,128,4,128]{3,1,2,0:T(8,128)(2,1)S(1)} %collective-permute-done) | copy-start | bytes 786436
  172.2 27.2 %collective-permute-start.1 = (bf16[2,128,4,128]{3,1,2,0:T(8,128)(2,1)S(1)}, bf16[2,128,4,128]{3,1,2,0:T(8,128)(2,1)S(1)}, u32[]{:S(2)}, u32[]{:S(2)}) collective-permute-start(bf16[2,128,4,128]{3,1,2,0:T(8,128)(2,1)S(1)} %pad_maximum_fusion.2), channel_id=1, source_target_pairs={{0,8},{4,12},{8,16},{12,20},{16,24},{20,28},{24,32},{28,36},{32,40... | collective-permute-start | bytes 786440 | tf_op jit(solution)/shard_map/ppermute | solution.py:24
  176.7 9.8 %copy-start.43 = (pred[128,128]{0,1:T(8,128)(4,1)S(1)}, pred[128,128]{0,1:T(8,128)(4,1)}, u32[]{:S(2)}) copy-start(pred[128,128]{0,1:T(8,128)(4,1)} %get-tuple-element.61) | copy-start | bytes 49156
  176.7 32.5 %copy-start.32 = (bf16[2,128,4,128]{3,1,2,0:T(8,128)(2,1)}, bf16[2,128,4,128]{3,1,2,0:T(8,128)(2,1)S(1)}, u32[]{:S(2)}) copy-start(bf16[2,128,4,128]{3,1,2,0:T(8,128)(2,1)S(1)} %collective-permute-done.2) | copy-start | bytes 786436
  177.5 33.7 %copy-start.33 = (bf16[2,128,4,128]{3,1,2,0:T(8,128)(2,1)}, bf16[2,128,4,128]{3,1,2,0:T(8,128)(2,1)S(1)}, u32[]{:S(2)}) copy-start(bf16[2,128,4,128]{3,1,2,0:T(8,128)(2,1)S(1)} %collective-permute-done.3) | copy-start | bytes 786436
  177.9 21.5 %copy-start.42 = (pred[128,128]{0,1:T(8,128)(4,1)S(1)}, pred[128,128]{0,1:T(8,128)(4,1)}, u32[]{:S(2)}) copy-start(pred[128,128]{0,1:T(8,128)(4,1)} %get-tuple-element.58) | copy-start | bytes 49156
  186.5 26.7 %copy-start.35 = (bf16[2,128,4,128]{3,1,2,0:T(8,128)(2,1)}, bf16[2,128,4,128]{3,1,2,0:T(8,128)(2,1)S(1)}, u32[]{:S(2)}) copy-start(bf16[2,128,4,128]{3,1,2,0:T(8,128)(2,1)S(1)} %collective-permute-done.4) | copy-start | bytes 786436
  199.0 16.3 %copy-start.37 = (bf16[2,128,4,128]{3,1,2,0:T(8,128)(2,1)}, bf16[2,128,4,128]{3,1,2,0:T(8,128)(2,1)S(1)}, u32[]{:S(2)}) copy-start(bf16[2,128,4,128]{3,1,2,0:T(8,128)(2,1)S(1)} %collective-permute-done.5) | copy-start | bytes 786436
  199.4 7.9 %copy-start.30 = (bf16[2,128,4,128]{3,1,2,0:T(8,128)(2,1)}, bf16[2,128,4,128]{3,1,2,0:T(8,128)(2,1)S(1)}, u32[]{:S(2)}) copy-start(bf16[2,128,4,128]{3,1,2,0:T(8,128)(2,1)S(1)} %collective-permute-done.1) | copy-start | bytes 786436
  205.6 2.3 copy-start.6
  206.0 10.8 %collective-permute-start.6 = (bf16[2,128,4,128]{3,1,2,0:T(8,128)(2,1)S(1)}, bf16[2,128,4,128]{3,1,2,0:T(8,128)(2,1)S(1)}, u32[]{:S(2)}, u32[]{:S(2)}) collective-permute-start(bf16[2,128,4,128]{3,1,2,0:T(8,128)(2,1)S(1)} %pad_maximum_fusion.3), channel_id=1, source_target_pairs={{4,0},{8,4},{12,8},{16,12},{20,16},{24,20},{28,24},{32,28},{36,32}... | collective-permute-start | bytes 786440 | tf_op jit(solution)/shard_map/ppermute | solution.py:24
  208.0 20.6 %collective-permute-start.7 = (bf16[2,128,4,128]{3,1,2,0:T(8,128)(2,1)S(1)}, bf16[2,128,4,128]{3,1,2,0:T(8,128)(2,1)S(1)}, u32[]{:S(2)}, u32[]{:S(2)}) collective-permute-start(bf16[2,128,4,128]{3,1,2,0:T(8,128)(2,1)S(1)} %pad_maximum_fusion.4), channel_id=1, source_target_pairs={{8,0},{12,4},{16,8},{20,12},{24,16},{28,20},{32,24},{36,28},{40,32... | collective-permute-start | bytes 786440 | tf_op jit(solution)/shard_map/ppermute | solution.py:24
  209.9 27.9 %collective-permute-start.8 = (bf16[2,128,4,128]{3,1,2,0:T(8,128)(2,1)S(1)}, bf16[2,128,4,128]{3,1,2,0:T(8,128)(2,1)S(1)}, u32[]{:S(2)}, u32[]{:S(2)}) collective-permute-start(bf16[2,128,4,128]{3,1,2,0:T(8,128)(2,1)S(1)} %pad_maximum_fusion.5), channel_id=1, source_target_pairs={{12,0},{16,4},{20,8},{24,12},{28,16},{32,20},{36,24},{40,28},{44,3... | collective-permute-start | bytes 786440 | tf_op jit(solution)/shard_map/ppermute | solution.py:24
  211.5 2.3 copy-start
  211.9 25.9 %collective-permute-start.9 = (bf16[2,128,4,128]{3,1,2,0:T(8,128)(2,1)S(1)}, bf16[2,128,4,128]{3,1,2,0:T(8,128)(2,1)S(1)}, u32[]{:S(2)}, u32[]{:S(2)}) collective-permute-start(bf16[2,128,4,128]{3,1,2,0:T(8,128)(2,1)S(1)} %pad_maximum_fusion.6), channel_id=1, source_target_pairs={{16,0},{20,4},{24,8},{28,12},{32,16},{36,20},{40,24},{44,28},{48,3... | collective-permute-start | bytes 786440 | tf_op jit(solution)/shard_map/ppermute | solution.py:24
  213.5 2.4 copy-start.2
  213.8 2.6 copy-start.18
  213.8 23.9 %collective-permute-start.10 = (bf16[2,128,4,128]{3,1,2,0:T(8,128)(2,1)S(1)}, bf16[2,128,4,128]{3,1,2,0:T(8,128)(2,1)S(1)}, u32[]{:S(2)}, u32[]{:S(2)}) collective-permute-start(bf16[2,128,4,128]{3,1,2,0:T(8,128)(2,1)S(1)} %pad_maximum_fusion.7), channel_id=1, source_target_pairs={{20,0},{24,4},{28,8},{32,12},{36,16},{40,20},{44,24},{48,28},{52,3... | collective-permute-start | bytes 786440 | tf_op jit(solution)/shard_map/ppermute | solution.py:24
  216.8 34.4 %collective-permute-start.11 = (bf16[2,128,4,128]{3,1,2,0:T(8,128)(2,1)S(1)}, bf16[2,128,4,128]{3,1,2,0:T(8,128)(2,1)S(1)}, u32[]{:S(2)}, u32[]{:S(2)}) collective-permute-start(bf16[2,128,4,128]{3,1,2,0:T(8,128)(2,1)S(1)} %pad_maximum_fusion.8), channel_id=1, source_target_pairs={{24,0},{28,4},{32,8},{36,12},{40,16},{44,20},{48,24},{52,28},{56,3... | collective-permute-start | bytes 786440 | tf_op jit(solution)/shard_map/ppermute | solution.py:24
  218.4 33.8 %copy-start.21 = (f32[128,64]{1,0:T(8,128)S(1)}, f32[128,64]{1,0:T(8,128)}, u32[]{:S(2)}) copy-start(f32[128,64]{1,0:T(8,128)} %copy-done.19) | copy-start | bytes 98308
  218.4 33.8 %copy-start.25 = (f32[128,64]{1,0:T(8,128)S(1)}, f32[128,64]{1,0:T(8,128)}, u32[]{:S(2)}) copy-start(f32[128,64]{1,0:T(8,128)} %copy-done.23) | copy-start | bytes 98308
  218.7 33.6 %copy-start.52 = (f32[1,128]{1,0:T(1,128)S(1)}, f32[1,128]{1,0:T(1,128)}, u32[]{:S(2)}) copy-start(f32[1,128]{1,0:T(1,128)} %param.15) | copy-start | bytes 1540
  251.4 2.3 copy-start.28
  251.5 2.3 copy-start.48
  251.5 2.3 copy-start.49
  251.5 2.3 copy-start.50
  254.7 133.6 %reduce-scatter.7.cloned.1.call-start = ((), (), s32[]{:S(2)}) async-start(), calls=%async_computation.7 | async-start | bytes 2359296
  342.0 3.0 copy-start.1
  342.0 3.0 copy-start.34
  342.7 3.7 copy-start.3
  342.7 3.7 copy-start.36
  345.0 2.7 copy-start.5
  345.0 2.7 copy-start.38
  346.4 2.7 copy-start.7
  346.4 2.7 copy-start.40
  347.7 2.7 copy-start.55
  347.7 2.7 copy-start.56
  352.7 3.7 copy-start.9
  352.7 3.7 copy-start.31
  352.7 18.0 %all-to-all-start.1 = ((bf16[8,128,512]{2,1,0:T(8,128)(2,1)}), bf16[8,128,512]{2,1,0:T(8,128)(2,1)S(1)}, u32[]{:S(2)}, u32[]{:S(2)}) async-start(bf16[8,128,512]{2,1,0:T(8,128)(2,1)} %bitcast.588), calls=%async_computation.2 | async-start | bytes 2097152 | tf_op jit(solution)/shard_map/all_to_all | solution.py:217
  360.5 4.0 %copy-start.22 = (f32[128,64]{1,0:T(8,128)S(1)}, f32[128,64]{1,0:T(8,128)}, u32[]{:S(2)}) copy-start(f32[128,64]{1,0:T(8,128)} %copy-done.19) | copy-start | bytes 98308
  360.5 4.0 %copy-start.26 = (f32[128,64]{1,0:T(8,128)S(1)}, f32[128,64]{1,0:T(8,128)}, u32[]{:S(2)}) copy-start(f32[128,64]{1,0:T(8,128)} %copy-done.23) | copy-start | bytes 98308
  370.8 3.9 copy-start.12
  370.8 3.9 copy-start.13
  371.9 16.5 %collective-permute-start.12 = (bf16[128,4096]{1,0:T(8,128)(2,1)}, bf16[128,4096]{1,0:T(8,128)(2,1)}, u32[]{:S(2)}, u32[]{:S(2)}) collective-permute-start(bf16[128,4096]{1,0:T(8,128)(2,1)} %bitcast.231), channel_id=1, source_target_pairs={{0,3},{1,0},{2,1},{3,2},{4,7},{5,4},{6,5},{7,6},{8,11},{9,8},{10,9... | collective-permute-start | bytes 3145736 | tf_op jit(solution)/shard_map/ppermute | solution.py:29
  376.6 3.7 copy-start.10
  376.6 3.7 copy-start.11
  (11 other events, 12.9 us)
Sparse Core Ops, SparseCore 0:
  10.3 37.8 all-gather.2
  52.9 91.6 reduce-scatter.4
  254.8 79.0 all-gather.4
  341.5 38.8 reduce-scatter.6
where the time goes:
time: 401 us; the launch traced here: 400 us
  waiting for transfers between devices  234 us (58%)
  starting transfers between devices  42.2 us (11%)
  matrix products  34.7 us (9%)
  local copies, waits for them, and re-layouts  34.6 us (9%)
  blocking collectives  22.6 us (6%)
  other arithmetic  16.6 us (4%)
  between operations  15 us (4%)
    reduce_scatter x1, waiting for transfers between devices, local(): lax.psum_scatter(jnp.dot(inputs_slice, weight_slice, preferred_element_ty...  83.1 us
    all_gather x1, waiting for transfers between devices, local(): group_back = lax.all_gather(both_back, 'cb', axis=0, tiled=True)  74.3 us
    ppermute x12, waiting for transfers between devices, passed_along(): return lax.ppermute(block, axis, route)  53.6 us
    ppermute x12, starting transfers between devices, passed_along(): return lax.ppermute(block, axis, route)  35.4 us
    all_to_all x1, blocking collectives, local(): inputs_slice = lax.all_to_all(tokens_here, 'cb', 1, 0, tiled=True)  22.6 us
    unnamed x125, local copies, waits for them, and re-layouts  17.4 us
    all_gather x1, waiting for transfers between devices, local(): weight_slice = lax.all_gather(both_rows, 'cz', axis=0, tiled=True)  14.6 us
    dot_general x7, matrix products, grad_block(): jnp.einsum('grqk,kgd->qgrd', score_grad, key_pair[0], preferred_element_t...  11.1 us
  transfers between devices with their start and end apart: 18, of which 11 were waited for; matrix products, arithmetic and copies ran while one was open for 13% of the time, Pallas kernels for 0%

commit v1 on v0

--- a/solution.py
+++ b/solution.py
@@ -88,7 +88,10 @@
     ctx_index = lax.axis_index("cb") * col_parts + col_index
     both_rows = jnp.concatenate([w_key[0], w_value[0]], 1)
     weight_slice = lax.all_gather(both_rows, "cz", axis=0, tiled=True)
-    inputs_slice = lax.all_to_all(tokens_here, "cb", 1, 0, tiled=True)
+    size = lax.axis_size("cb")
+    tiles = jnp.stack(jnp.split(tokens_here, size, axis=1), axis=0)
+    tiles = lax.all_to_all(tiles, "cb", split_axis=0, concat_axis=0)
+    inputs_slice = jnp.concatenate(tiles, axis=0)
     projected = lax.psum_scatter(
         jnp.dot(inputs_slice, weight_slice, preferred_element_type=jnp.float32),
         "cb",

time: 401 us -> 407 us (1.015)
  matrix products: 34.7 us -> 47.3 us
  waiting for transfers between devices: 234 us -> 222 us
    ppermute x12, waiting for transfers between devices: 53.6 us -> 47.8 us  [passed_along(): return lax.ppermute(block, axis, route)]
    all_gather x1, waiting for transfers between devices: 14.6 us -> 9.48 us  [local(): weight_slice = lax.all_gather(both_rows, 'cz', axis=0, tiled=True)]
    mul x4 -> x6, local copies, waits for them, and re-layouts: 6.15 us -> 8.73 us  [normalize_back(): values * cubed * jnp.mean(values * scaled, -1, keepdims=True)]
    unnamed x125 -> x98, local copies, waits for them, and re-layouts: 17.4 us -> 16.8 us
  transfers between devices with their start and end apart: 18 -> 18, of which waited for: 11 -> 10; matrix products, arithmetic and copies ran while one was open for 13% -> 16% of each run, Pallas kernels for 0% -> 0%
where the time goes in v1:
time: 407 us; the launch traced here: 405 us
  waiting for transfers between devices  222 us (55%)
  matrix products  47.3 us (12%)
  starting transfers between devices  42.9 us (11%)
  local copies, waits for them, and re-layouts  38.1 us (9%)
  blocking collectives  22.6 us (6%)
  other arithmetic  17.1 us (4%)
  between operations  14.9 us (4%)
    reduce_scatter x1, waiting for transfers between devices, local(): lax.psum_scatter(jnp.dot(inputs_slice, weight_slice, preferred_element_ty...  85.1 us
    all_gather x1, waiting for transfers between devices, local(): group_back = lax.all_gather(both_back, 'cb', axis=0, tiled=True)  71.8 us
    ppermute x12, waiting for transfers between devices, passed_along(): return lax.ppermute(block, axis, route)  47.8 us
    ppermute x12, starting transfers between devices, passed_along(): return lax.ppermute(block, axis, route)  36.1 us
    all_to_all x1, blocking collectives, local(): tiles = lax.all_to_all(tiles, 'cb', split_axis=0, concat_axis=0)  22.6 us
    unnamed x98, local copies, waits for them, and re-layouts  16.8 us
    dot_general x7, matrix products, grad_block(): jnp.einsum('grqk,kgd->qgrd', score_grad, key_pair[0], preferred_element_t...  14 us
    all_gather x1, waiting for transfers between devices, local(): weight_slice = lax.all_gather(both_rows, 'cz', axis=0, tiled=True)  9.48 us
  transfers between devices with their start and end apart: 18, of which 10 were waited for; matrix products, arithmetic and copies ran while one was open for 16% of the time, Pallas kernels for 0%

profile of v1, /device:TPU:1, one launch (start us, length us, event | category | flops | bytes accessed | tf_op | source)
XLA Modules:
  0.0 405.1 jit_solution(5108274174484886151)
XLA Ops:
  7.2 1.5 pad_maximum_fusion.11
  16.2 22.6 %all_to_all.24 = bf16[8,128,512]{2,1,0:T(8,128)(2,1)S(1)} all-to-all(bf16[8,128,512]{2,1,0:T(8,128)(2,1)S(1)} %fusion.98), channel_id=1, replica_groups=mesh['cb'=8,'cz'=8,'pipe'=4] {'cb'}, dimensions={0} | all-to-all | bytes 2097152 | tf_op jit(solution)/shard_map/all_to_all | solution.py:93
  38.8 9.5 %all-gather.3.cloned.1.call-done = bf16[512,1024]{1,0:T(8,128)(2,1)} async-done(((bf16[64,1024]{1,0:T(8,128)(2,1)}), bf16[512,1024]{1,0:T(8,128)(2,1)}) %all-gather.3.cloned.1.call-update) | async-done | bytes 1048592 | tf_op jit(solution)/shard_map/all_gather | solution.py:90
  48.3 4.5 %fusion.157 = f32[1024,1024]{1,0:T(8,128)} fusion(bf16[1024,512]{1,0:T(8,128)(2,1)S(1)} %bitcast.610, bf16[512,1024]{1,0:T(8,128)(2,1)} %all-gather.3.cloned.1.call-done), kind=kOutput, calls=%fused_computation.305 | convolution fusion | flops 1073741824 | bytes 6291456 | tf_op jit(solution)/shard_map/dot_general | solution.py:96
  59.3 85.1 %reduce-scatter.3.cloned.1.call-done = f32[128,1024]{1,0:T(8,128)} async-done(((f32[1024,1024]{1,0:T(8,128)}), f32[128,1024]{1,0:T(8,128)}) %reduce-scatter.3.cloned.1.call-update) | async-done | bytes 524304 | tf_op jit(solution)/shard_map/reduce_scatter | solution.py:95
  144.5 1.1 convert.86
  146.4 1.2 multiply_reduce_fusion.2
  148.9 3.9 collective-permute-start
  152.8 5.7 %collective-permute-start.2 = (bf16[2,128,4,128]{3,1,2,0:T(8,128)(2,1)}, bf16[2,128,4,128]{3,1,2,0:T(8,128)(2,1)S(1)}, u32[]{:S(2)}, u32[]{:S(2)}) collective-permute-start(bf16[2,128,4,128]{3,1,2,0:T(8,128)(2,1)} %pad_maximum_fusion.2), channel_id=1, source_target_pairs={{0,12},{4,16},{8,20},{12,24},{16,28},{20,32},{24,36},{28,40},{32,4... | collective-permute-start | bytes 786440 | tf_op jit(solution)/shard_map/ppermute | solution.py:24
  158.5 2.9 collective-permute-start.3
  161.3 6.2 %collective-permute-start.4 = (bf16[2,128,4,128]{3,1,2,0:T(8,128)(2,1)}, bf16[2,128,4,128]{3,1,2,0:T(8,128)(2,1)}, u32[]{:S(2)}, u32[]{:S(2)}) collective-permute-start(bf16[2,128,4,128]{3,1,2,0:T(8,128)(2,1)} %pad_maximum_fusion.2), channel_id=1, source_target_pairs={{0,20},{4,24},{8,28},{12,32},{16,36},{20,40},{24,44},{28,48},{32,5... | collective-permute-start | bytes 786440 | tf_op jit(solution)/shard_map/ppermute | solution.py:24
  167.5 6.1 %collective-permute-start.5 = (bf16[2,128,4,128]{3,1,2,0:T(8,128)(2,1)}, bf16[2,128,4,128]{3,1,2,0:T(8,128)(2,1)}, u32[]{:S(2)}, u32[]{:S(2)}) collective-permute-start(bf16[2,128,4,128]{3,1,2,0:T(8,128)(2,1)} %pad_maximum_fusion.2), channel_id=1, source_target_pairs={{0,24},{4,28},{8,32},{12,36},{16,40},{20,44},{24,48},{28,52},{32,5... | collective-permute-start | bytes 786440 | tf_op jit(solution)/shard_map/ppermute | solution.py:24
  175.7 3.5 collective-permute-start.1
  179.2 1.3 fusion.156
  180.9 1.3 fusion.152
  182.2 5.5 %collective-permute-done.4 = bf16[2,128,4,128]{3,1,2,0:T(8,128)(2,1)} collective-permute-done((bf16[2,128,4,128]{3,1,2,0:T(8,128)(2,1)}, bf16[2,128,4,128]{3,1,2,0:T(8,128)(2,1)}, u32[]{:S(2)}, u32[]{:S(2)}) %collective-permute-start.4) | collective-permute-done | bytes 262176 | tf_op jit(solution)/shard_map/ppermute | solution.py:24
  187.7 1.3 fusion.151
  189.0 11.5 %collective-permute-done.5 = bf16[2,128,4,128]{3,1,2,0:T(8,128)(2,1)} collective-permute-done((bf16[2,128,4,128]{3,1,2,0:T(8,128)(2,1)}, bf16[2,128,4,128]{3,1,2,0:T(8,128)(2,1)}, u32[]{:S(2)}, u32[]{:S(2)}) %collective-permute-start.5) | collective-permute-done | bytes 262176 | tf_op jit(solution)/shard_map/ppermute | solution.py:24
  200.5 1.3 fusion.150
  205.7 1.3 fusion.111
  207.0 1.3 fusion.112
  208.2 1.3 fusion.113
  209.5 1.3 convolution_add_fusion.3
  211.4 1.2 fusion.47
  212.9 1.3 collective-permute-start.6
  214.9 1.3 collective-permute-start.7
  216.8 1.3 collective-permute-start.8
  218.1 1.2 fusion.50
  219.7 1.3 collective-permute-start.9
  221.0 1.2 fusion.51
  222.6 1.4 collective-permute-start.10
  224.0 1.2 fusion.52
  226.4 1.3 collective-permute-start.11
  228.3 7.1 %collective-permute-done.7 = bf16[2,128,4,128]{3,1,2,0:T(8,128)(2,1)S(1)} collective-permute-done((bf16[2,128,4,128]{3,1,2,0:T(8,128)(2,1)S(1)}, bf16[2,128,4,128]{3,1,2,0:T(8,128)(2,1)S(1)}, u32[]{:S(2)}, u32[]{:S(2)}) %collective-permute-start.7) | collective-permute-done | bytes 262176 | tf_op jit(solution)/shard_map/ppermute | solution.py:24
  235.4 9.3 %collective-permute-done.8 = bf16[2,128,4,128]{3,1,2,0:T(8,128)(2,1)S(1)} collective-permute-done((bf16[2,128,4,128]{3,1,2,0:T(8,128)(2,1)S(1)}, bf16[2,128,4,128]{3,1,2,0:T(8,128)(2,1)S(1)}, u32[]{:S(2)}, u32[]{:S(2)}) %collective-permute-start.8) | collective-permute-done | bytes 262176 | tf_op jit(solution)/shard_map/ppermute | solution.py:24
  244.6 14.4 %collective-permute-done.11 = bf16[2,128,4,128]{3,1,2,0:T(8,128)(2,1)S(1)} collective-permute-done((bf16[2,128,4,128]{3,1,2,0:T(8,128)(2,1)S(1)}, bf16[2,128,4,128]{3,1,2,0:T(8,128)(2,1)S(1)}, u32[]{:S(2)}, u32[]{:S(2)}) %collective-permute-start.11) | collective-permute-done | bytes 262176 | tf_op jit(solution)/shard_map/ppermute | solution.py:24
  263.5 1.2 mul.517
  264.6 1.1 mul.518
  265.8 1.3 mul.597
  267.1 2.3 mul.598
  269.4 71.8 %all-gather.5.cloned.1.call-done = bf16[1024,1024]{1,0:T(8,128)(2,1)} async-done(((bf16[128,1024]{1,0:T(8,128)(2,1)}), bf16[1024,1024]{1,0:T(8,128)(2,1)}) %all-gather.5.cloned.1.call-update) | async-done | bytes 2097168 | tf_op jit(solution)/shard_map/all_gather | solution.py:208
  341.3 4.2 %fusion.159 = f32[512,1024]{1,0:T(8,128)} fusion(bf16[1024,512]{1,0:T(8,128)(2,1)S(1)} %bitcast.611, bf16[1024,1024]{1,0:T(8,128)(2,1)} %all-gather.5.cloned.1.call-done), kind=kOutput, calls=%fused_computation.307 | convolution fusion | flops 1073741824 | bytes 5242880 | tf_op jit(solution)/shard_map/dot_general | solution.py:210
  346.8 1.4 fusion.106
  348.2 2.3 fusion.107
  350.5 2.3 fusion.108
  352.8 2.4 fusion.109
  355.1 2.2 convolution_add_fusion.1
  357.3 2.3 convolution_convert_fusion
  359.6 3.7 all-to-all-start.1
  363.3 3.0 fusion.12
  366.4 1.1 fusion.149
  367.5 1.6 copy.455
  369.1 2.4 copy.456
  371.5 2.8 multiply_add_fusion
  374.3 3.4 all-to-all-done.1
  377.7 1.1 copy.462
  378.8 2.7 collective-permute-start.12
  382.2 1.3 mul.602
  383.5 2.5 mul.603
  386.0 1.1 concatenate.52
  387.2 2.9 fusion.88
  390.1 4.5 %collective-permute-done.12 = bf16[128,4096]{1,0:T(8,128)(2,1)} collective-permute-done((bf16[128,4096]{1,0:T(8,128)(2,1)}, bf16[128,4096]{1,0:T(8,128)(2,1)}, u32[]{:S(2)}, u32[]{:S(2)}) %collective-permute-start.12) | collective-permute-done | bytes 1048608 | tf_op jit(solution)/shard_map/ppermute | solution.py:29
  394.6 1.7 slice_bitcast_fusion.1
  396.2 2.3 copy.484
  (195 shorter events, 33.1 us)
Async XLA Ops:
  7.2 41.1 %all-gather.3.cloned.1.call-start = ((), (), s32[]{:S(2)}) async-start(), calls=%async_computation.4 | async-start | bytes 1179648 | tf_op jit(solution)/shard_map/all_gather | solution.py:90
  8.8 135.7 %reduce-scatter.3.cloned.1.call-start = ((), (), s32[]{:S(2)}) async-start(), calls=%async_computation.5 | async-start | bytes 4718592 | tf_op jit(solution)/shard_map/reduce_scatter | solution.py:95
  38.8 13.9 %copy-start.10 = (bf16[8,128,512]{2,1,0:T(8,128)(2,1)}, bf16[8,128,512]{2,1,0:T(8,128)(2,1)S(1)}, u32[]{:S(2)}) copy-start(bf16[8,128,512]{2,1,0:T(8,128)(2,1)S(1)} %all_to_all.24) | copy-start | bytes 3145732
  52.8 1.0 copy-start.18
  52.8 288.5 %all-gather.5.cloned.1.call-start = ((), (), s32[]{:S(2)}) async-start(), calls=%async_computation.6 | async-start | bytes 2359296 | tf_op jit(solution)/shard_map/all_gather | solution.py:208
  53.9 1.6 copy-start.40
  54.8 1.8 copy-start.20
  54.8 1.8 copy-start.24
  55.5 0.6 copy-start.36
  56.1 1.0 copy-start.37
  56.8 2.0 copy-start.39
  58.8 89.0 %copy-start.21 = (f32[128,64]{1,0:T(8,128)S(1)}, f32[128,64]{1,0:T(8,128)}, u32[]{:S(2)}) copy-start(f32[128,64]{1,0:T(8,128)} %copy-done.20) | copy-start | bytes 98308
  58.8 89.0 %copy-start.25 = (f32[128,64]{1,0:T(8,128)S(1)}, f32[128,64]{1,0:T(8,128)}, u32[]{:S(2)}) copy-start(f32[128,64]{1,0:T(8,128)} %copy-done.24) | copy-start | bytes 98308
  145.5 2.1 copy-start.28
  148.0 32.5 %copy-start.16 = (bf16[128,4,64]{2,0,1:T(8,128)(2,1)}, bf16[128,4,64]{2,0,1:T(8,128)(2,1)S(1)}, u32[]{:S(2)}) copy-start(bf16[128,4,64]{2,0,1:T(8,128)(2,1)S(1)} %get-tuple-element.17) | copy-start | bytes 196612
  148.9 26.8 %collective-permute-start = (bf16[2,128,4,128]{3,1,2,0:T(8,128)(2,1)}, bf16[2,128,4,128]{3,1,2,0:T(8,128)(2,1)}, u32[]{:S(2)}, u32[]{:S(2)}) collective-permute-start(bf16[2,128,4,128]{3,1,2,0:T(8,128)(2,1)} %pad_maximum_fusion.2), channel_id=1, source_target_pairs={{0,4},{4,8},{8,12},{12,16},{16,20},{20,24},{24,28},{28,32},{32,36}... | collective-permute-start | bytes 786440 | tf_op jit(solution)/shard_map/ppermute | solution.py:24
  152.8 27.7 %collective-permute-start.2 = (bf16[2,128,4,128]{3,1,2,0:T(8,128)(2,1)}, bf16[2,128,4,128]{3,1,2,0:T(8,128)(2,1)S(1)}, u32[]{:S(2)}, u32[]{:S(2)}) collective-permute-start(bf16[2,128,4,128]{3,1,2,0:T(8,128)(2,1)} %pad_maximum_fusion.2), channel_id=1, source_target_pairs={{0,12},{4,16},{8,20},{12,24},{16,28},{20,32},{24,36},{28,40},{32,4... | collective-permute-start | bytes 786440 | tf_op jit(solution)/shard_map/ppermute | solution.py:24
  158.5 22.4 %collective-permute-start.3 = (bf16[2,128,4,128]{3,1,2,0:T(8,128)(2,1)}, bf16[2,128,4,128]{3,1,2,0:T(8,128)(2,1)}, u32[]{:S(2)}, u32[]{:S(2)}) collective-permute-start(bf16[2,128,4,128]{3,1,2,0:T(8,128)(2,1)} %pad_maximum_fusion.2), channel_id=1, source_target_pairs={{0,16},{4,20},{8,24},{12,28},{16,32},{20,36},{24,40},{28,44},{32,4... | collective-permute-start | bytes 786440 | tf_op jit(solution)/shard_map/ppermute | solution.py:24
  161.3 26.4 %collective-permute-start.4 = (bf16[2,128,4,128]{3,1,2,0:T(8,128)(2,1)}, bf16[2,128,4,128]{3,1,2,0:T(8,128)(2,1)}, u32[]{:S(2)}, u32[]{:S(2)}) collective-permute-start(bf16[2,128,4,128]{3,1,2,0:T(8,128)(2,1)} %pad_maximum_fusion.2), channel_id=1, source_target_pairs={{0,20},{4,24},{8,28},{12,32},{16,36},{20,40},{24,44},{28,48},{32,5... | collective-permute-start | bytes 786440 | tf_op jit(solution)/shard_map/ppermute | solution.py:24
  167.5 33.0 %collective-permute-start.5 = (bf16[2,128,4,128]{3,1,2,0:T(8,128)(2,1)}, bf16[2,128,4,128]{3,1,2,0:T(8,128)(2,1)}, u32[]{:S(2)}, u32[]{:S(2)}) collective-permute-start(bf16[2,128,4,128]{3,1,2,0:T(8,128)(2,1)} %pad_maximum_fusion.2), channel_id=1, source_target_pairs={{0,24},{4,28},{8,32},{12,36},{16,40},{20,44},{24,48},{28,52},{32,5... | collective-permute-start | bytes 786440 | tf_op jit(solution)/shard_map/ppermute | solution.py:24
  174.5 30.5 %copy-start.30 = (bf16[128,4,128,1]{0,2,3,1:T(8,128)(2,1)}, bf16[128,4,128,1]{0,2,3,1:T(8,128)(2,1)S(1)}, u32[]{:S(2)}) copy-start(bf16[128,4,128,1]{0,2,3,1:T(8,128)(2,1)S(1)} %copy.342) | copy-start | bytes 393220
  175.7 26.1 %collective-permute-start.1 = (bf16[2,128,4,128]{3,1,2,0:T(8,128)(2,1)}, bf16[2,128,4,128]{3,1,2,0:T(8,128)(2,1)S(1)}, u32[]{:S(2)}, u32[]{:S(2)}) collective-permute-start(bf16[2,128,4,128]{3,1,2,0:T(8,128)(2,1)} %pad_maximum_fusion.2), channel_id=1, source_target_pairs={{0,8},{4,12},{8,16},{12,20},{16,24},{20,28},{24,32},{28,36},{32,40... | collective-permute-start | bytes 786440 | tf_op jit(solution)/shard_map/ppermute | solution.py:24
  180.5 35.7 %copy-start.34 = (bf16[2,128,4,128]{3,1,2,0:T(8,128)(2,1)}, bf16[2,128,4,128]{3,1,2,0:T(8,128)(2,1)S(1)}, u32[]{:S(2)}) copy-start(bf16[2,128,4,128]{3,1,2,0:T(8,128)(2,1)S(1)} %collective-permute-done.2) | copy-start | bytes 786436
  201.8 12.4 %copy-start.32 = (bf16[2,128,4,128]{3,1,2,0:T(8,128)(2,1)}, bf16[2,128,4,128]{3,1,2,0:T(8,128)(2,1)S(1)}, u32[]{:S(2)}) copy-start(bf16[2,128,4,128]{3,1,2,0:T(8,128)(2,1)S(1)} %collective-permute-done.1) | copy-start | bytes 786436
  212.6 2.3 copy-start.6
  212.9 13.5 %collective-permute-start.6 = (bf16[2,128,4,128]{3,1,2,0:T(8,128)(2,1)S(1)}, bf16[2,128,4,128]{3,1,2,0:T(8,128)(2,1)S(1)}, u32[]{:S(2)}, u32[]{:S(2)}) collective-permute-start(bf16[2,128,4,128]{3,1,2,0:T(8,128)(2,1)S(1)} %pad_maximum_fusion.3), channel_id=1, source_target_pairs={{4,0},{8,4},{12,8},{16,12},{20,16},{24,20},{28,24},{32,28},{36,32}... | collective-permute-start | bytes 786440 | tf_op jit(solution)/shard_map/ppermute | solution.py:24
  214.5 2.3 copy-start.8
  214.9 20.5 %collective-permute-start.7 = (bf16[2,128,4,128]{3,1,2,0:T(8,128)(2,1)S(1)}, bf16[2,128,4,128]{3,1,2,0:T(8,128)(2,1)S(1)}, u32[]{:S(2)}, u32[]{:S(2)}) collective-permute-start(bf16[2,128,4,128]{3,1,2,0:T(8,128)(2,1)S(1)} %pad_maximum_fusion.4), channel_id=1, source_target_pairs={{8,0},{12,4},{16,8},{20,12},{24,16},{28,20},{32,24},{36,28},{40,32... | collective-permute-start | bytes 786440 | tf_op jit(solution)/shard_map/ppermute | solution.py:24
  216.8 27.8 %collective-permute-start.8 = (bf16[2,128,4,128]{3,1,2,0:T(8,128)(2,1)S(1)}, bf16[2,128,4,128]{3,1,2,0:T(8,128)(2,1)S(1)}, u32[]{:S(2)}, u32[]{:S(2)}) collective-permute-start(bf16[2,128,4,128]{3,1,2,0:T(8,128)(2,1)S(1)} %pad_maximum_fusion.5), channel_id=1, source_target_pairs={{12,0},{16,4},{20,8},{24,12},{28,16},{32,20},{36,24},{40,28},{44,3... | collective-permute-start | bytes 786440 | tf_op jit(solution)/shard_map/ppermute | solution.py:24
  219.3 3.2 copy-start
  219.7 25.0 %collective-permute-start.9 = (bf16[2,128,4,128]{3,1,2,0:T(8,128)(2,1)S(1)}, bf16[2,128,4,128]{3,1,2,0:T(8,128)(2,1)S(1)}, u32[]{:S(2)}, u32[]{:S(2)}) collective-permute-start(bf16[2,128,4,128]{3,1,2,0:T(8,128)(2,1)S(1)} %pad_maximum_fusion.6), channel_id=1, source_target_pairs={{16,0},{20,4},{24,8},{28,12},{32,16},{36,20},{40,24},{44,28},{48,3... | collective-permute-start | bytes 786440 | tf_op jit(solution)/shard_map/ppermute | solution.py:24
  222.2 3.3 copy-start.2
  222.5 3.5 copy-start.31
  222.6 22.1 %collective-permute-start.10 = (bf16[2,128,4,128]{3,1,2,0:T(8,128)(2,1)S(1)}, bf16[2,128,4,128]{3,1,2,0:T(8,128)(2,1)S(1)}, u32[]{:S(2)}, u32[]{:S(2)}) collective-permute-start(bf16[2,128,4,128]{3,1,2,0:T(8,128)(2,1)S(1)} %pad_maximum_fusion.7), channel_id=1, source_target_pairs={{20,0},{24,4},{28,8},{32,12},{36,16},{40,20},{44,24},{48,28},{52,3... | collective-permute-start | bytes 786440 | tf_op jit(solution)/shard_map/ppermute | solution.py:24
  225.2 0.8 copy-start.4
  226.4 32.6 %collective-permute-start.11 = (bf16[2,128,4,128]{3,1,2,0:T(8,128)(2,1)S(1)}, bf16[2,128,4,128]{3,1,2,0:T(8,128)(2,1)S(1)}, u32[]{:S(2)}, u32[]{:S(2)}) collective-permute-start(bf16[2,128,4,128]{3,1,2,0:T(8,128)(2,1)S(1)} %pad_maximum_fusion.8), channel_id=1, source_target_pairs={{24,0},{28,4},{32,8},{36,12},{40,16},{44,20},{48,24},{52,28},{56,3... | collective-permute-start | bytes 786440 | tf_op jit(solution)/shard_map/ppermute | solution.py:24
  228.0 31.4 %copy-start.22 = (f32[128,64]{1,0:T(8,128)S(1)}, f32[128,64]{1,0:T(8,128)}, u32[]{:S(2)}) copy-start(f32[128,64]{1,0:T(8,128)} %copy-done.20) | copy-start | bytes 98308
  228.0 31.4 %copy-start.26 = (f32[128,64]{1,0:T(8,128)S(1)}, f32[128,64]{1,0:T(8,128)}, u32[]{:S(2)}) copy-start(f32[128,64]{1,0:T(8,128)} %copy-done.24) | copy-start | bytes 98308
  259.3 3.0 copy-start.29
  262.4 3.3 copy-start.38
  263.2 131.4 %reduce-scatter.5.cloned.1.call-start = ((), (), s32[]{:S(2)}) async-start(), calls=%async_computation.7 | async-start | bytes 2359296 | tf_op jit(solution)/shard_map/reduce_scatter | solution.py:209
  265.8 75.5 %copy-start.11 = (bf16[8,128,512]{2,1,0:T(8,128)(2,1)S(1)}, bf16[8,128,512]{2,1,0:T(8,128)(2,1)}, u32[]{:S(2)}) copy-start(bf16[8,128,512]{2,1,0:T(8,128)(2,1)} %copy-done.10) | copy-start | bytes 3145732
  345.5 0.9 copy-start.17
  345.5 1.3 copy-start.35
  345.5 2.7 copy-start.1
  346.8 3.7 copy-start.3
  348.2 4.5 %copy-start.5 = (bf16[4,4,128,128]{2,3,1,0:T(8,128)(2,1)S(1)}, bf16[4,4,128,128]{2,3,1,0:T(8,128)(2,1)}, u32[]{:S(2)}) copy-start(bf16[4,4,128,128]{2,3,1,0:T(8,128)(2,1)} %copy-done.4) | copy-start | bytes 1572868
  350.5 4.6 %copy-start.7 = (bf16[4,4,128,128]{2,3,1,0:T(8,128)(2,1)S(1)}, bf16[4,4,128,128]{2,3,1,0:T(8,128)(2,1)}, u32[]{:S(2)}) copy-start(bf16[4,4,128,128]{2,3,1,0:T(8,128)(2,1)} %copy-done.6) | copy-start | bytes 1572868
  352.8 4.6 %copy-start.19 = (bf16[1024,1024]{1,0:T(8,128)(2,1)S(1)}, bf16[1024,1024]{1,0:T(8,128)(2,1)}, u32[]{:S(2)}) copy-start(bf16[1024,1024]{1,0:T(8,128)(2,1)} %all-gather.5.cloned.1.call-done) | copy-start | bytes 6291460
  352.8 4.6 %copy-start.41 = (bf16[512,1024]{1,0:T(8,128)(2,1)S(1)}, bf16[512,1024]{1,0:T(8,128)(2,1)}, u32[]{:S(2)}) copy-start(bf16[512,1024]{1,0:T(8,128)(2,1)} %all-gather.3.cloned.1.call-done) | copy-start | bytes 3145732
  359.6 3.7 copy-start.9
  359.6 3.7 copy-start.33
  359.6 18.1 %all-to-all-start.1 = ((bf16[8,128,512]{2,1,0:T(8,128)(2,1)}), bf16[8,128,512]{2,1,0:T(8,128)(2,1)S(1)}, u32[]{:S(2)}, u32[]{:S(2)}) async-start(bf16[8,128,512]{2,1,0:T(8,128)(2,1)} %bitcast.629), calls=%async_computation.3 | async-start | bytes 2097152 | tf_op jit(solution)/shard_map/all_to_all | solution.py:220
  367.5 4.0 copy-start.23
  367.5 4.0 copy-start.27
  377.7 3.8 copy-start.14
  377.7 3.8 copy-start.15
  378.8 15.8 %collective-permute-start.12 = (bf16[128,4096]{1,0:T(8,128)(2,1)}, bf16[128,4096]{1,0:T(8,128)(2,1)}, u32[]{:S(2)}, u32[]{:S(2)}) collective-permute-start(bf16[128,4096]{1,0:T(8,128)(2,1)} %bitcast.226), channel_id=1, source_target_pairs={{0,3},{1,0},{2,1},{3,2},{4,7},{5,4},{6,5},{7,6},{8,11},{9,8},{10,9... | collective-permute-start | bytes 3145736 | tf_op jit(solution)/shard_map/ppermute | solution.py:29
  383.5 3.7 copy-start.12
  383.5 3.7 copy-start.13
Sparse Core Ops, SparseCore 0:
  10.3 37.9 all-gather.2
  52.9 91.5 reduce-scatter.2
  263.3 77.9 all-gather.4
  345.6 38.6 reduce-scatter.4
